TPU v7x, 128 devices: a whole 4x4x4 slice. The times are simulated.
128 devices in a mesh: month: 4 (over x), grid: 32 (over y, z, core).
Axes of the slice: x: 4, y: 4, z: 4, core: 2. Of those that a mesh axis runs over, the one named last changes fastest.
Arguments:
- tracers: float32 [64, 32768], P(None, 'grid'), may hold values from 0.25 to 7
- targets: float32 [64], replicated, may hold values from 0.5 to 2
- retain: float32 [8, 32768], P('month', 'grid'), may hold values from 0.5 to 0.95
- blocks: float32 [8, 256, 8, 128, 128], P('month', 'grid'), may hold values from 3.90625e-07 to 0.00390625
- cols: int32 [8, 256, 8], P('month', 'grid'), may hold values from 0 to 255, as said below
Outputs:
- spun_up: float32 [64, 32768], P('month', 'grid')
Inputs may be any that keep to these rules, and one draw needn't show every extreme that they name: cols[m, i, 0] = i; for 1 <= k < 6, cols[m, i, k] names a block on the same grid device as block i (block b lies on device b // 8); the last 2 entries name blocks on other devices, and of the 16 such entries of one device's block rows in one month at most 1 lie on any single device, exactly 1 on some.
All inputs are finite; a program needn't handle non-finite values.
Results may differ from a plain program's by a relative error of at most 0.0001.
Values sent between devices are 32-bit elements; how exact they have to be, the bound alone decides.
No kernel may reach another device: no remote copies, remote signals or barrier semaphores. Data moves between devices by JAX's collectives and lax.ppermute only.
A program may use at most 64 MiB of HBM per device.

v0:
```python
import jax
import jax.numpy as jnp
from jax import lax
from jax.sharding import PartitionSpec as P


def passed_along(value, axis, by):
    devices = lax.axis_size(axis)
    return lax.ppermute(value, axis, [(i, (i + by) % devices) for i in range(devices)])


def local(tracers, targets, retain, blocks, cols):
    sections = lax.axis_size("month")
    devices = lax.axis_size("grid")
    section = lax.axis_index("month")
    months_here = blocks.shape[0]
    blk_count = blocks.shape[1]
    blk_size = blocks.shape[3]
    rows_here = blk_count * blk_size
    batch = tracers.shape[0] // sections
    points = rows_here * devices
    held = jnp.zeros((batch, rows_here), jnp.float32)
    kept = jnp.zeros((batch, rows_here), jnp.float32)
    last_step = max(2 * sections - 2, 3 * sections - 4)
    for step in range(last_step + 1):
        if step < sections:
            held = jnp.where(section == 0, tracers[step * batch : (step + 1) * batch], held)
        if step < 2 * sections - 1:
            working = (step - section >= 0) & (step - section < sections)
            apply_state = held
            for apply_month_idx in range(months_here):
                whole = lax.all_gather(apply_state, "grid", axis=1, tiled=True)
                picked = whole.reshape(batch, -1, blk_size)[:, cols[apply_month_idx]]
                mixed = jnp.einsum(
                    "tbkc,bkrc->tbr",
                    picked,
                    blocks[apply_month_idx],
                    precision=lax.Precision.HIGHEST,
                    preferred_element_type=jnp.float32,
                )
                apply_state = retain[apply_month_idx][None, :] * apply_state + mixed.reshape(
                    batch, rows_here
                )
            held = jnp.where(working, apply_state, held)
            finished = step - sections + 1
            if finished >= 0:
                inventory = lax.psum(jnp.sum(held, axis=1), "grid")
                goal = targets[finished * batch : (finished + 1) * batch]
                scaled = held * (goal * points / inventory)[:, None]
                held = jnp.where(section == sections - 1, scaled, held)
        arrived = jnp.where(
            section == sections - 1, step == 2 * sections - 2, step == sections + 2 * section
        )
        kept = jnp.where(arrived, held, kept)
        if step < last_step:
            held = passed_along(held, "month", 1)
    return kept


def solution(mesh):
    return jax.shard_map(
        local,
        mesh=mesh,
        in_specs=(
            P(None, "grid"),
            P(),
            P("month", "grid"),
            P("month", "grid", None, None, None),
            P("month", "grid", None),
        ),
        out_specs=P("month", "grid"),
        check_vma=False,
    )
```

profile of v0, /device:TPU:0, one launch (start us, length us, event | category | flops | bytes accessed | tf_op | source)
XLA Modules:
  0.0 1031.2 jit_solution(10049208585597531722)
XLA Ops:
  9.7 46.3 %all-gather.15.cloned.1.call-done = f32[16,32768]{1,0:T(8,128)} async-done(((f32[16,1024]{1,0:T(8,128)}), f32[16,32768]{1,0:T(8,128)}) %all-gather.15.cloned.1.call-update) | async-done | bytes 2097168 | tf_op jit(solution)/shard_map/all_gather | solution.py:32
  56.0 1.7 copy_bitcast_fusion.13
  58.4 5.3 fusion.42
  64.6 43.0 %all-gather.17.cloned.1.call-done = f32[16,32768]{1,0:T(8,128)} async-done(((f32[16,1024]{1,0:T(8,128)}), f32[16,32768]{1,0:T(8,128)}) %all-gather.17.cloned.1.call-update) | async-done | bytes 2097168 | tf_op jit(solution)/shard_map/all_gather | solution.py:32
  107.6 1.7 copy_bitcast_fusion.12
  110.0 5.3 fusion.63
  116.9 4.0 collective-permute-done
  121.6 41.9 %all-gather.19.cloned.1.call-done = f32[16,32768]{1,0:T(8,128)} async-done(((f32[16,1024]{1,0:T(8,128)}), f32[16,32768]{1,0:T(8,128)}) %all-gather.19.cloned.1.call-update) | async-done | bytes 2097168 | tf_op jit(solution)/shard_map/all_gather | solution.py:32
  163.5 1.7 copy_bitcast_fusion.11
  166.0 5.3 fusion.45
  172.0 43.1 %all-gather.21.cloned.1.call-done = f32[16,32768]{1,0:T(8,128)} async-done(((f32[16,1024]{1,0:T(8,128)}), f32[16,32768]{1,0:T(8,128)}) %all-gather.21.cloned.1.call-update) | async-done | bytes 2097168 | tf_op jit(solution)/shard_map/all_gather | solution.py:32
  215.1 1.7 copy_bitcast_fusion.10
  217.5 5.3 fusion.66
  224.4 4.0 collective-permute-done.1
  229.2 41.9 %all-gather.23.cloned.1.call-done = f32[16,32768]{1,0:T(8,128)} async-done(((f32[16,1024]{1,0:T(8,128)}), f32[16,32768]{1,0:T(8,128)}) %all-gather.23.cloned.1.call-update) | async-done | bytes 2097168 | tf_op jit(solution)/shard_map/all_gather | solution.py:32
  271.1 1.7 copy_bitcast_fusion.9
  273.5 5.3 fusion.48
  279.7 42.9 %all-gather.25.cloned.1.call-done = f32[16,32768]{1,0:T(8,128)} async-done(((f32[16,1024]{1,0:T(8,128)}), f32[16,32768]{1,0:T(8,128)}) %all-gather.25.cloned.1.call-update) | async-done | bytes 2097168 | tf_op jit(solution)/shard_map/all_gather | solution.py:32
  325.1 5.3 fusion.69
  332.0 4.0 collective-permute-done.2
  336.7 41.9 %all-gather.27.cloned.1.call-done = f32[16,32768]{1,0:T(8,128)} async-done(((f32[16,1024]{1,0:T(8,128)}), f32[16,32768]{1,0:T(8,128)}) %all-gather.27.cloned.1.call-update) | async-done | bytes 2097168 | tf_op jit(solution)/shard_map/all_gather | solution.py:32
  381.0 5.3 fusion.51
  387.1 43.1 %all-gather.29.cloned.1.call-done = f32[16,32768]{1,0:T(8,128)} async-done(((f32[16,1024]{1,0:T(8,128)}), f32[16,32768]{1,0:T(8,128)}) %all-gather.29.cloned.1.call-update) | async-done | bytes 2097168 | tf_op jit(solution)/shard_map/all_gather | solution.py:32
  430.2 1.7 copy_bitcast_fusion.6
  432.6 5.3 fusion.72
  438.1 65.2 %psum.28 = f32[16]{0:T(128)S(1)} all-reduce(f32[16]{0:T(128)S(1)} %get-tuple-element.11), channel_id=1, replica_groups=mesh['month'=4,'grid'=32] {'grid'}, use_global_device_ids=true, to_apply=%region_1.2 | all-reduce | flops 16 | bytes 128 | tf_op jit(solution)/shard_map/psum | solution.py:47
  504.8 4.0 collective-permute-done.3
  509.5 38.9 %all-gather.31.cloned.1.call-done = f32[16,32768]{1,0:T(8,128)} async-done(((f32[16,1024]{1,0:T(8,128)}), f32[16,32768]{1,0:T(8,128)}) %all-gather.31.cloned.1.call-update) | async-done | bytes 2097168 | tf_op jit(solution)/shard_map/all_gather | solution.py:32
  550.8 5.3 fusion.54
  556.9 43.1 %all-gather.33.cloned.1.call-done = f32[16,32768]{1,0:T(8,128)} async-done(((f32[16,1024]{1,0:T(8,128)}), f32[16,32768]{1,0:T(8,128)}) %all-gather.33.cloned.1.call-update) | async-done | bytes 2097168 | tf_op jit(solution)/shard_map/all_gather | solution.py:32
  602.4 5.3 fusion.75
  607.9 65.2 %psum.29 = f32[16]{0:T(128)S(1)} all-reduce(f32[16]{0:T(128)S(1)} %get-tuple-element.9), channel_id=1, replica_groups=mesh['month'=4,'grid'=32] {'grid'}, use_global_device_ids=true, to_apply=%region_3.4 | all-reduce | flops 16 | bytes 128 | tf_op jit(solution)/shard_map/psum | solution.py:47
  674.7 4.0 collective-permute-done.4
  679.6 38.7 %all-gather.35.cloned.1.call-done = f32[16,32768]{1,0:T(8,128)} async-done(((f32[16,1024]{1,0:T(8,128)}), f32[16,32768]{1,0:T(8,128)}) %all-gather.35.cloned.1.call-update) | async-done | bytes 2097168 | tf_op jit(solution)/shard_map/all_gather | solution.py:32
  720.7 5.3 fusion.57
  726.8 43.1 %all-gather.37.cloned.1.call-done = f32[16,32768]{1,0:T(8,128)} async-done(((f32[16,1024]{1,0:T(8,128)}), f32[16,32768]{1,0:T(8,128)}) %all-gather.37.cloned.1.call-update) | async-done | bytes 2097168 | tf_op jit(solution)/shard_map/all_gather | solution.py:32
  769.9 1.7 copy_bitcast_fusion.2
  772.3 5.3 fusion.78
  777.8 65.2 %psum.30 = f32[16]{0:T(128)S(1)} all-reduce(f32[16]{0:T(128)S(1)} %get-tuple-element.7), channel_id=1, replica_groups=mesh['month'=4,'grid'=32] {'grid'}, use_global_device_ids=true, to_apply=%region_5.6 | all-reduce | flops 16 | bytes 128 | tf_op jit(solution)/shard_map/psum | solution.py:47
  844.6 4.0 collective-permute-done.5
  849.3 38.9 %all-gather.39.cloned.1.call-done = f32[16,32768]{1,0:T(8,128)} async-done(((f32[16,1024]{1,0:T(8,128)}), f32[16,32768]{1,0:T(8,128)}) %all-gather.39.cloned.1.call-update) | async-done | bytes 2097168 | tf_op jit(solution)/shard_map/all_gather | solution.py:32
  888.2 1.7 copy_bitcast_fusion.1
  890.6 5.3 fusion.60
  896.6 43.2 %all-gather.41.cloned.1.call-done = f32[16,32768]{1,0:T(8,128)} async-done(((f32[16,1024]{1,0:T(8,128)}), f32[16,32768]{1,0:T(8,128)}) %all-gather.41.cloned.1.call-update) | async-done | bytes 2097168 | tf_op jit(solution)/shard_map/all_gather | solution.py:32
  942.2 5.3 fusion.81
  947.6 65.2 %psum.31 = f32[16]{0:T(128)S(1)} all-reduce(f32[16]{0:T(128)S(1)} %get-tuple-element.5), channel_id=1, replica_groups=mesh['month'=4,'grid'=32] {'grid'}, use_global_device_ids=true, to_apply=%region_7.8 | all-reduce | flops 16 | bytes 128 | tf_op jit(solution)/shard_map/psum | solution.py:47
  1014.4 4.0 collective-permute-done.6
  1019.0 5.0 collective-permute-done.7
  (125 shorter events, 45.1 us)
Async XLA Ops:
  6.5 49.5 %all-gather.15.cloned.1.call-start = ((), (), s32[]{:S(2)}) async-start(), calls=%async_computation | async-start | bytes 2162688 | tf_op jit(solution)/shard_map/all_gather | solution.py:32
  8.0 99.6 %all-gather.17.cloned.1.call-start = ((), (), s32[]{:S(2)}) async-start(), calls=%async_computation.1 | async-start | bytes 2162688 | tf_op jit(solution)/shard_map/all_gather | solution.py:32
  58.4 5.3 copy-start.3
  64.4 99.1 %all-gather.19.cloned.1.call-start = ((), (), s32[]{:S(2)}) async-start(), calls=%async_computation.2 | async-start | bytes 2162688 | tf_op jit(solution)/shard_map/all_gather | solution.py:32
  110.0 5.3 copy-start.10
  115.4 5.5 collective-permute-start
  121.6 93.6 %all-gather.21.cloned.1.call-start = ((), (), s32[]{:S(2)}) async-start(), calls=%async_computation.3 | async-start | bytes 2162688 | tf_op jit(solution)/shard_map/all_gather | solution.py:32
  165.9 5.3 copy-start.1
  172.0 99.1 %all-gather.23.cloned.1.call-start = ((), (), s32[]{:S(2)}) async-start(), calls=%async_computation.4 | async-start | bytes 2162688 | tf_op jit(solution)/shard_map/all_gather | solution.py:32
  217.5 5.3 copy-start.15
  222.9 5.5 collective-permute-start.1
  229.1 93.6 %all-gather.25.cloned.1.call-start = ((), (), s32[]{:S(2)}) async-start(), calls=%async_computation.5 | async-start | bytes 2162688 | tf_op jit(solution)/shard_map/all_gather | solution.py:32
  273.5 5.3 copy-start.2
  279.5 99.1 %all-gather.27.cloned.1.call-start = ((), (), s32[]{:S(2)}) async-start(), calls=%async_computation.6 | async-start | bytes 2162688 | tf_op jit(solution)/shard_map/all_gather | solution.py:32
  325.1 5.3 copy-start.16
  330.4 5.5 collective-permute-start.2
  336.7 93.6 %all-gather.29.cloned.1.call-start = ((), (), s32[]{:S(2)}) async-start(), calls=%async_computation.7 | async-start | bytes 2162688 | tf_op jit(solution)/shard_map/all_gather | solution.py:32
  381.0 5.3 copy-start
  387.0 161.4 %all-gather.31.cloned.1.call-start = ((), (), s32[]{:S(2)}) async-start(), calls=%async_computation.8 | async-start | bytes 2162688 | tf_op jit(solution)/shard_map/all_gather | solution.py:32
  432.6 5.3 copy-start.11
  432.6 70.6 %copy-start.17 = (f32[64]{0:T(128)S(1)}, f32[64]{0:T(128)}, u32[]{:S(2)}) copy-start(f32[64]{0:T(128)} %param.6) | copy-start | bytes 772
  503.3 5.5 collective-permute-start.3
  508.8 0.6 copy-start.6
  509.5 90.5 %all-gather.33.cloned.1.call-start = ((), (), s32[]{:S(2)}) async-start(), calls=%async_computation.9 | async-start | bytes 2162688 | tf_op jit(solution)/shard_map/all_gather | solution.py:32
  550.8 5.3 copy-start.7
  556.8 161.5 %all-gather.35.cloned.1.call-start = ((), (), s32[]{:S(2)}) async-start(), calls=%async_computation.10 | async-start | bytes 2162688 | tf_op jit(solution)/shard_map/all_gather | solution.py:32
  602.4 5.3 copy-start.13
  673.2 5.5 collective-permute-start.4
  678.7 0.6 copy-start.8
  679.4 90.5 %all-gather.37.cloned.1.call-start = ((), (), s32[]{:S(2)}) async-start(), calls=%async_computation.11 | async-start | bytes 2162688 | tf_op jit(solution)/shard_map/all_gather | solution.py:32
  720.7 5.3 copy-start.9
  726.7 161.5 %all-gather.39.cloned.1.call-start = ((), (), s32[]{:S(2)}) async-start(), calls=%async_computation.12 | async-start | bytes 2162688 | tf_op jit(solution)/shard_map/all_gather | solution.py:32
  772.3 5.3 copy-start.14
  843.1 5.5 collective-permute-start.5
  848.6 0.6 copy-start.4
  849.2 90.5 %all-gather.41.cloned.1.call-start = ((), (), s32[]{:S(2)}) async-start(), calls=%async_computation.13 | async-start | bytes 2162688 | tf_op jit(solution)/shard_map/all_gather | solution.py:32
  890.6 5.3 copy-start.5
  942.2 5.3 copy-start.12
  1013.0 5.5 collective-permute-start.6
  1018.5 5.5 collective-permute-start.7
Sparse Core Ops, SparseCore 0:
  9.7 46.2 all-gather.14
  64.5 43.0 all-gather.16
  121.7 41.8 all-gather.18
  172.1 43.0 all-gather.20
  229.2 41.8 all-gather.22
  279.6 43.0 all-gather.24
  336.8 41.8 all-gather.26
  387.2 43.0 all-gather.28
  509.6 38.7 all-gather.30
  557.0 43.0 all-gather.32
  679.5 38.7 all-gather.34
  726.8 43.0 all-gather.36
  849.4 38.7 all-gather.38
  896.7 43.0 all-gather.40
where the time goes:
time: 1030 us
  waiting for transfers between devices  623 us (60%)
  blocking collectives  261 us (25%)
  matrix products  74.5 us (7%)
  local copies, waits for them, and re-layouts  36.2 us (4%)
  between operations  13.7 us (1%)
  starting transfers between devices  12 us (1%)
  other arithmetic  10.6 us (1%)
    all_gather x14, waiting for transfers between devices, local(): whole = lax.all_gather(apply_state, 'grid', axis=1, tiled=True)  590 us
    psum x4, blocking collectives, local(): inventory = lax.psum(jnp.sum(held, axis=1), 'grid')  261 us
    dot_general x14, matrix products, local(): jnp.einsum('tbkc,bkrc->tbr', picked, blocks[apply_month_idx], precision=l...  74.5 us
    ppermute x8, waiting for transfers between devices, passed_along(): lax.ppermute(value, axis, [(i, (i + by) % devices) for i in range(devices)])  33 us
    reshape x14, local copies, waits for them, and re-layouts, local(): picked = whole.reshape(batch, -1, blk_size)[:, cols[apply_month_idx]]  24.5 us
  transfers between devices with their start and end apart: 22, of which 22 were waited for; matrix products, arithmetic and copies ran while one was open for 0% of the time, Pallas kernels for 0%

commit v1 on v0

--- a/solution.py
+++ b/solution.py
@@ -44,7 +44,7 @@
             held = jnp.where(working, apply_state, held)
             finished = step - sections + 1
             if finished >= 0:
-                inventory = lax.psum(jnp.sum(held, axis=1), "grid")
+                inventory = jnp.sum(lax.all_gather(jnp.sum(held, axis=1), "grid"), axis=0)
                 goal = targets[finished * batch : (finished + 1) * batch]
                 scaled = held * (goal * points / inventory)[:, None]
                 held = jnp.where(section == sections - 1, scaled, held)

time: 1030 us -> 1030 us (level)
    psum x4 -> x0, blocking collectives: 261 us -> none  [local(): inventory = lax.psum(jnp.sum(held, axis=1), 'grid')]
    unnamed x0 -> x4, blocking collectives: none -> 261 us
where the time goes in v1:
time: 1030 us
  waiting for transfers between devices  622 us (60%)
  blocking collectives  261 us (25%)
  matrix products  74.5 us (7%)
  local copies, waits for them, and re-layouts  38.2 us (4%)
  between operations  14.5 us (1%)
  starting transfers between devices  12 us (1%)
  other arithmetic  10.7 us (1%)
    all_gather x14, waiting for transfers between devices, local(): whole = lax.all_gather(apply_state, 'grid', axis=1, tiled=True)  589 us
    unnamed x4, blocking collectives  261 us
    dot_general x14, matrix products, local(): jnp.einsum('tbkc,bkrc->tbr', picked, blocks[apply_month_idx], precision=l...  74.5 us
    ppermute x8, waiting for transfers between devices, passed_along(): lax.ppermute(value, axis, [(i, (i + by) % devices) for i in range(devices)])  33 us
    reshape x14, local copies, waits for them, and re-layouts, local(): picked = whole.reshape(batch, -1, blk_size)[:, cols[apply_month_idx]]  24.5 us
  transfers between devices with their start and end apart: 22, of which 22 were waited for; matrix products, arithmetic and copies ran while one was open for 0% of the time, Pallas kernels for 0%

profile of v1, /device:TPU:0, one launch (start us, length us, event | category | flops | bytes accessed | tf_op | source)
XLA Modules:
  0.0 1032.6 jit_solution(3975576434973537787)
XLA Ops:
  9.7 46.3 %all-gather.19.cloned.1.call-done = f32[16,32768]{1,0:T(8,128)} async-done(((f32[16,1024]{1,0:T(8,128)}), f32[16,32768]{1,0:T(8,128)}) %all-gather.19.cloned.1.call-update) | async-done | bytes 2097168 | tf_op jit(solution)/shard_map/all_gather | solution.py:32
  56.0 1.7 copy_bitcast_fusion.13
  58.4 5.3 fusion.42
  64.6 43.0 %all-gather.21.cloned.1.call-done = f32[16,32768]{1,0:T(8,128)} async-done(((f32[16,1024]{1,0:T(8,128)}), f32[16,32768]{1,0:T(8,128)}) %all-gather.21.cloned.1.call-update) | async-done | bytes 2097168 | tf_op jit(solution)/shard_map/all_gather | solution.py:32
  107.6 1.7 copy_bitcast_fusion.12
  110.0 5.3 fusion.63
  116.9 4.0 collective-permute-done
  121.6 41.9 %all-gather.23.cloned.1.call-done = f32[16,32768]{1,0:T(8,128)} async-done(((f32[16,1024]{1,0:T(8,128)}), f32[16,32768]{1,0:T(8,128)}) %all-gather.23.cloned.1.call-update) | async-done | bytes 2097168 | tf_op jit(solution)/shard_map/all_gather | solution.py:32
  163.5 1.7 copy_bitcast_fusion.11
  166.0 5.3 fusion.45
  172.0 43.1 %all-gather.25.cloned.1.call-done = f32[16,32768]{1,0:T(8,128)} async-done(((f32[16,1024]{1,0:T(8,128)}), f32[16,32768]{1,0:T(8,128)}) %all-gather.25.cloned.1.call-update) | async-done | bytes 2097168 | tf_op jit(solution)/shard_map/all_gather | solution.py:32
  215.1 1.7 copy_bitcast_fusion.10
  217.5 5.3 fusion.66
  224.4 4.0 collective-permute-done.1
  229.2 41.9 %all-gather.27.cloned.1.call-done = f32[16,32768]{1,0:T(8,128)} async-done(((f32[16,1024]{1,0:T(8,128)}), f32[16,32768]{1,0:T(8,128)}) %all-gather.27.cloned.1.call-update) | async-done | bytes 2097168 | tf_op jit(solution)/shard_map/all_gather | solution.py:32
  271.1 1.7 copy_bitcast_fusion.9
  273.5 5.3 fusion.48
  279.7 42.9 %all-gather.29.cloned.1.call-done = f32[16,32768]{1,0:T(8,128)} async-done(((f32[16,1024]{1,0:T(8,128)}), f32[16,32768]{1,0:T(8,128)}) %all-gather.29.cloned.1.call-update) | async-done | bytes 2097168 | tf_op jit(solution)/shard_map/all_gather | solution.py:32
  325.1 5.3 fusion.69
  332.0 4.0 collective-permute-done.2
  336.7 41.9 %all-gather.31.cloned.1.call-done = f32[16,32768]{1,0:T(8,128)} async-done(((f32[16,1024]{1,0:T(8,128)}), f32[16,32768]{1,0:T(8,128)}) %all-gather.31.cloned.1.call-update) | async-done | bytes 2097168 | tf_op jit(solution)/shard_map/all_gather | solution.py:32
  381.0 5.3 fusion.51
  388.4 41.8 %all-gather.33.cloned.1.call-done = f32[16,32768]{1,0:T(8,128)} async-done(((f32[16,1024]{1,0:T(8,128)}), f32[16,32768]{1,0:T(8,128)}) %all-gather.33.cloned.1.call-update) | async-done | bytes 2097168 | tf_op jit(solution)/shard_map/all_gather | solution.py:32
  432.6 5.3 fusion.72
  438.3 65.1 %all-reduce = f32[512]{0:T(512)S(1)} all-reduce(f32[512]{0:T(512)S(1)} %dynamic-update-slice), channel_id=2, replica_groups=mesh['month'=4,'grid'=32] {'grid'}, use_global_device_ids=true, to_apply=%add | all-reduce | flops 512 | bytes 4096
  505.2 4.0 collective-permute-done.3
  509.9 38.9 %all-gather.35.cloned.1.call-done = f32[16,32768]{1,0:T(8,128)} async-done(((f32[16,1024]{1,0:T(8,128)}), f32[16,32768]{1,0:T(8,128)}) %all-gather.35.cloned.1.call-update) | async-done | bytes 2097168 | tf_op jit(solution)/shard_map/all_gather | solution.py:32
  548.8 1.7 copy_bitcast_fusion.5
  551.2 5.3 fusion.54
  557.2 43.1 %all-gather.37.cloned.1.call-done = f32[16,32768]{1,0:T(8,128)} async-done(((f32[16,1024]{1,0:T(8,128)}), f32[16,32768]{1,0:T(8,128)}) %all-gather.37.cloned.1.call-update) | async-done | bytes 2097168 | tf_op jit(solution)/shard_map/all_gather | solution.py:32
  602.8 5.3 fusion.75
  608.5 65.1 %all-reduce.1 = f32[512]{0:T(512)S(1)} all-reduce(f32[512]{0:T(512)S(1)} %dynamic-update-slice.1), channel_id=3, replica_groups=mesh['month'=4,'grid'=32] {'grid'}, use_global_device_ids=true, to_apply=%add.1 | all-reduce | flops 512 | bytes 4096
  675.4 4.0 collective-permute-done.4
  680.3 38.7 %all-gather.39.cloned.1.call-done = f32[16,32768]{1,0:T(8,128)} async-done(((f32[16,1024]{1,0:T(8,128)}), f32[16,32768]{1,0:T(8,128)}) %all-gather.39.cloned.1.call-update) | async-done | bytes 2097168 | tf_op jit(solution)/shard_map/all_gather | solution.py:32
  721.4 5.3 fusion.57
  727.5 43.1 %all-gather.41.cloned.1.call-done = f32[16,32768]{1,0:T(8,128)} async-done(((f32[16,1024]{1,0:T(8,128)}), f32[16,32768]{1,0:T(8,128)}) %all-gather.41.cloned.1.call-update) | async-done | bytes 2097168 | tf_op jit(solution)/shard_map/all_gather | solution.py:32
  770.6 1.7 copy_bitcast_fusion.2
  773.0 5.3 fusion.78
  778.7 65.1 %all-reduce.2 = f32[512]{0:T(512)S(1)} all-reduce(f32[512]{0:T(512)S(1)} %dynamic-update-slice.2), channel_id=4, replica_groups=mesh['month'=4,'grid'=32] {'grid'}, use_global_device_ids=true, to_apply=%add.2 | all-reduce | flops 512 | bytes 4096
  845.6 4.0 collective-permute-done.5
  850.3 38.9 %all-gather.43.cloned.1.call-done = f32[16,32768]{1,0:T(8,128)} async-done(((f32[16,1024]{1,0:T(8,128)}), f32[16,32768]{1,0:T(8,128)}) %all-gather.43.cloned.1.call-update) | async-done | bytes 2097168 | tf_op jit(solution)/shard_map/all_gather | solution.py:32
  889.2 1.7 copy_bitcast_fusion.1
  891.6 5.3 fusion.60
  897.6 43.2 %all-gather.45.cloned.1.call-done = f32[16,32768]{1,0:T(8,128)} async-done(((f32[16,1024]{1,0:T(8,128)}), f32[16,32768]{1,0:T(8,128)}) %all-gather.45.cloned.1.call-update) | async-done | bytes 2097168 | tf_op jit(solution)/shard_map/all_gather | solution.py:32
  943.2 5.3 fusion.81
  948.9 65.1 %all-reduce.3 = f32[512]{0:T(512)S(1)} all-reduce(f32[512]{0:T(512)S(1)} %dynamic-update-slice.3), channel_id=5, replica_groups=mesh['month'=4,'grid'=32] {'grid'}, use_global_device_ids=true, to_apply=%add.3 | all-reduce | flops 512 | bytes 4096
  1015.8 4.0 collective-permute-done.6
  1020.3 5.0 collective-permute-done.7
  (144 shorter events, 47.1 us)
Async XLA Ops:
  6.5 49.5 %all-gather.19.cloned.1.call-start = ((), (), s32[]{:S(2)}) async-start(), calls=%async_computation | async-start | bytes 2162688 | tf_op jit(solution)/shard_map/all_gather | solution.py:32
  8.0 99.6 %all-gather.21.cloned.1.call-start = ((), (), s32[]{:S(2)}) async-start(), calls=%async_computation.1 | async-start | bytes 2162688 | tf_op jit(solution)/shard_map/all_gather | solution.py:32
  58.4 5.3 copy-start.3
  64.4 99.1 %all-gather.23.cloned.1.call-start = ((), (), s32[]{:S(2)}) async-start(), calls=%async_computation.2 | async-start | bytes 2162688 | tf_op jit(solution)/shard_map/all_gather | solution.py:32
  110.0 5.3 copy-start.11
  115.4 5.5 collective-permute-start
  121.6 93.6 %all-gather.25.cloned.1.call-start = ((), (), s32[]{:S(2)}) async-start(), calls=%async_computation.3 | async-start | bytes 2162688 | tf_op jit(solution)/shard_map/all_gather | solution.py:32
  165.9 5.3 copy-start.1
  172.0 99.1 %all-gather.27.cloned.1.call-start = ((), (), s32[]{:S(2)}) async-start(), calls=%async_computation.4 | async-start | bytes 2162688 | tf_op jit(solution)/shard_map/all_gather | solution.py:32
  217.5 5.3 copy-start.15
  222.9 5.5 collective-permute-start.1
  229.1 93.6 %all-gather.29.cloned.1.call-start = ((), (), s32[]{:S(2)}) async-start(), calls=%async_computation.5 | async-start | bytes 2162688 | tf_op jit(solution)/shard_map/all_gather | solution.py:32
  273.5 5.3 copy-start.2
  279.5 99.1 %all-gather.31.cloned.1.call-start = ((), (), s32[]{:S(2)}) async-start(), calls=%async_computation.6 | async-start | bytes 2162688 | tf_op jit(solution)/shard_map/all_gather | solution.py:32
  325.1 5.3 copy-start.16
  330.4 5.5 collective-permute-start.2
  336.7 93.6 %all-gather.33.cloned.1.call-start = ((), (), s32[]{:S(2)}) async-start(), calls=%async_computation.7 | async-start | bytes 2162688 | tf_op jit(solution)/shard_map/all_gather | solution.py:32
  381.0 5.3 copy-start
  381.0 6.1 copy-start.18
  387.0 161.7 %all-gather.35.cloned.1.call-start = ((), (), s32[]{:S(2)}) async-start(), calls=%async_computation.8 | async-start | bytes 2162688 | tf_op jit(solution)/shard_map/all_gather | solution.py:32
  432.6 5.3 copy-start.10
  432.6 71.0 %copy-start.17 = (f32[64]{0:T(128)S(1)}, f32[64]{0:T(128)}, u32[]{:S(2)}) copy-start(f32[64]{0:T(128)} %param.6) | copy-start | bytes 772
  503.7 5.5 collective-permute-start.3
  509.2 0.6 copy-start.6
  509.8 90.5 %all-gather.37.cloned.1.call-start = ((), (), s32[]{:S(2)}) async-start(), calls=%async_computation.9 | async-start | bytes 2162688 | tf_op jit(solution)/shard_map/all_gather | solution.py:32
  551.2 5.3 copy-start.7
  557.2 161.8 %all-gather.39.cloned.1.call-start = ((), (), s32[]{:S(2)}) async-start(), calls=%async_computation.10 | async-start | bytes 2162688 | tf_op jit(solution)/shard_map/all_gather | solution.py:32
  602.8 5.3 copy-start.13
  673.9 5.5 collective-permute-start.4
  679.4 0.6 copy-start.8
  680.0 90.5 %all-gather.41.cloned.1.call-start = ((), (), s32[]{:S(2)}) async-start(), calls=%async_computation.11 | async-start | bytes 2162688 | tf_op jit(solution)/shard_map/all_gather | solution.py:32
  721.4 5.3 copy-start.9
  727.4 161.8 %all-gather.43.cloned.1.call-start = ((), (), s32[]{:S(2)}) async-start(), calls=%async_computation.12 | async-start | bytes 2162688 | tf_op jit(solution)/shard_map/all_gather | solution.py:32
  773.0 5.3 copy-start.14
  844.1 5.5 collective-permute-start.5
  849.6 0.6 copy-start.4
  850.3 90.5 %all-gather.45.cloned.1.call-start = ((), (), s32[]{:S(2)}) async-start(), calls=%async_computation.13 | async-start | bytes 2162688 | tf_op jit(solution)/shard_map/all_gather | solution.py:32
  891.6 5.3 copy-start.5
  943.2 5.3 copy-start.12
  1014.3 5.5 collective-permute-start.6
  1019.8 5.5 collective-permute-start.7
Sparse Core Ops, SparseCore 0:
  9.7 46.2 all-gather.18
  64.5 43.0 all-gather.20
  121.7 41.8 all-gather.22
  172.1 43.0 all-gather.24
  229.2 41.8 all-gather.26
  279.6 43.0 all-gather.28
  336.8 41.8 all-gather.30
  387.2 43.0 all-gather.32
  509.9 38.7 all-gather.34
  557.3 43.0 all-gather.36
  680.2 38.7 all-gather.38
  727.5 43.0 all-gather.40
  850.4 38.7 all-gather.42
  897.8 43.0 all-gather.44
